TPU v7x, 256 devices: a whole 4x4x8 slice. The times are simulated.
256 devices in a mesh: seq: 16 (over y, x), fsdp: 16 (over z, core).
Axes of the slice: x: 4, y: 4, z: 8, core: 2. Of those that a mesh axis runs over, the one named last changes fastest.
Arguments:
- byte_rows: bfloat16 [16, 16384, 512], P('fsdp', 'seq'), may hold values from -6 to 6
- cotangent: bfloat16 [16, 16384, 512], P('fsdp', 'seq'), may hold values from -6 to 6
- doc_ids: int32 [16, 16384], P('fsdp', 'seq'), may hold values from 0 to 31, never falling along the last dimension, each value on 1 to 2048 neighbouring positions
- conv_weight: bfloat16 [8, 32, 16, 16], replicated, may hold values from -0.5 to 0.5
- norm_gain: float32 [512], replicated, may hold values from 0.5 to 1.5
- proj_weight: bfloat16 [4096, 512], P('fsdp'), may hold values from -0.25 to 0.25
- round_seed: int32 [1], replicated, may hold values from 0 to 1073741823
- step_count: int32 [1], replicated, may hold values from 0 to 999999
Outputs:
- grad_bytes: float32 [16, 16384, 512], P('fsdp', 'seq')
- grad_proj: float32 [4096, 512], P('fsdp')
- grad_conv: float32 [8, 32, 16, 16], replicated
- grad_gain: float32 [512], replicated
Inputs may be any that keep to these rules, and one draw needn't show every extreme that they name: `doc_ids`: along each sequence the document numbers never fall; no document covers more than 2048 bytes, and one covers exactly 2048.
All inputs are finite; a program needn't handle non-finite values.
Results may differ from a plain program's by a relative error of at most 0.0046.
Values may be sent and summed in bfloat16 or wider, within the bound.
No kernel may reach another device: no remote copies, remote signals or barrier semaphores. Data moves between devices by JAX's collectives and lax.ppermute only.
A program may use at most 128 MiB of HBM per device.

v0:
```python
import math

import jax
import jax.numpy as jnp
from jax import lax
from jax.sharding import PartitionSpec as P

GROUPS = 32
KERNEL = 8
STRIDE = 4
CG = 16


GELU_A = 0.7978845608028654
GELU_B = 0.044715
QUANT = 0.25


def shifted(value, axis, steps):
    count = lax.axis_size(axis)
    initial, last = (max(0, -steps), min(count, count - steps))
    return lax.ppermute(value, axis, [(source, source + steps) for source in range(initial, last)])


def gelu_grad(values):
    tangent = jnp.tanh(GELU_A * (values + GELU_B * values * values * values))
    return 0.5 * (1.0 + tangent) + 0.5 * values * (1.0 - tangent * tangent) * GELU_A * (
        1.0 + 3.0 * GELU_B * values * values
    )


def mix_bits(flat_index, seed_value, step_value):
    hashed = (
        flat_index * jnp.int32(-1640531535)
        + seed_value * jnp.int32(-2048144777)
        + step_value * jnp.int32(-1028477379)
    )
    hashed = hashed ^ lax.shift_right_logical(hashed, jnp.int32(16))
    hashed = hashed * jnp.int32(2146121005)
    hashed = hashed ^ lax.shift_right_logical(hashed, jnp.int32(15))
    hashed = hashed * jnp.int32(-2073254261)
    hashed = hashed ^ lax.shift_right_logical(hashed, jnp.int32(16))
    return lax.shift_right_logical(hashed, jnp.int32(8)).astype(jnp.float32) / 16777216.0


def tap_windows(series, extra_rows, patches):
    joined = jnp.concatenate([series, extra_rows], 0)
    tail_shape = joined.shape[1:]
    lower = joined[:-STRIDE].reshape((patches, STRIDE) + tail_shape)
    upper = joined[STRIDE:].reshape((patches, STRIDE) + tail_shape)
    return jnp.concatenate([lower, upper], 1)


def per_device(
    byte_rows, cotangent, doc_ids, conv_weight, norm_gain, proj_weight, round_seed, step_count
):
    byte_block = byte_rows[0]
    upstream = cotangent[0]
    doc_block = doc_ids[0]
    length = byte_block.shape[0]
    row_width = byte_block.shape[1]
    patches = length // STRIDE
    panel_rows = proj_weight.shape[0]
    full_width = panel_rows * lax.axis_size("fsdp")
    next_bytes, next_up, next_docs = shifted(
        (byte_block[:STRIDE], upstream[:STRIDE], doc_block[:STRIDE]), "seq", -1
    )
    window = tap_windows(byte_block, next_bytes, patches)
    up_window = tap_windows(upstream, next_up, patches)
    doc_window = tap_windows(doc_block, next_docs, patches)
    is_last = lax.axis_index("seq") == lax.axis_size("seq") - 1
    patch_ids = lax.broadcasted_iota(jnp.int32, (patches, KERNEL), 0)
    tap_ids = lax.broadcasted_iota(jnp.int32, (patches, KERNEL), 1)
    spilled = is_last & (patch_ids == patches - 1) & (tap_ids >= STRIDE)
    keep_tap = (doc_window == doc_window[:, :1]) & jnp.logical_not(spilled)
    keep_f = keep_tap.astype(jnp.float32)[:, :, None]
    masked = window * keep_tap.astype(jnp.bfloat16)[:, :, None]
    grouped = masked.reshape(patches, KERNEL, GROUPS, CG)
    hidden = jnp.einsum(
        "pkgc,kgcd->pgd", grouped, conv_weight, preferred_element_type=jnp.float32
    ).reshape(patches, row_width)
    factor = lax.rsqrt(jnp.mean(hidden * hidden, axis=-1, keepdims=True) + 1e-06)
    normed = (hidden * factor * norm_gain).astype(jnp.bfloat16)
    contract_last = (((1,), (1,)), ((), ()))
    full_proj = lax.all_gather(proj_weight, "fsdp", axis=0, tiled=True)
    pre_act = lax.dot_general(normed, full_proj, contract_last, preferred_element_type=jnp.float32)
    grad_pre = (
        up_window.astype(jnp.float32)
        * keep_f
        * gelu_grad(pre_act.reshape(patches, KERNEL, row_width))
    )
    grad_pre = grad_pre.reshape(patches, full_width).astype(jnp.bfloat16)
    grad_norm = jnp.dot(grad_pre, full_proj, preferred_element_type=jnp.float32)
    contract_first = (((0,), (0,)), ((), ()))
    panel_part = lax.psum_scatter(
        lax.dot_general(grad_pre, normed, contract_first, preferred_element_type=jnp.float32),
        "fsdp",
        scatter_dimension=0,
        tiled=True,
    )
    proj_sum = lax.psum(panel_part, "seq")
    gain_part = jnp.sum(grad_norm * hidden * factor, axis=0)
    gained = norm_gain * grad_norm
    grad_hidden = factor * gained - hidden * factor * factor * factor * jnp.mean(
        gained * hidden, axis=-1, keepdims=True
    )
    grad_hidden = grad_hidden.reshape(patches, GROUPS, CG)
    grouped_f = grouped.astype(jnp.float32)
    conv_f = conv_weight.astype(jnp.float32)
    conv_part = jnp.einsum(
        "pkgc,pgd->kgcd", grouped_f, grad_hidden, precision=lax.Precision.HIGHEST
    )
    gain_sum, conv_sum = lax.psum((gain_part, conv_part), ("seq", "fsdp"))
    grad_window = jnp.einsum("pgd,kgcd->pkgc", grad_hidden, conv_f, precision=lax.Precision.HIGHEST)
    grad_window = grad_window.reshape(patches, KERNEL, row_width) * keep_f
    back_lower = grad_window[:, :STRIDE].reshape(length, row_width)
    back_upper = grad_window[:, STRIDE:].reshape(length, row_width)
    incoming = shifted(back_upper[length - STRIDE :], "seq", 1)
    back_rows = back_lower + jnp.concatenate([incoming, back_upper[: length - STRIDE]], 0)
    grad_bytes = (upstream.astype(jnp.float32) + back_rows)[None]
    total_patches = patches * lax.axis_size("seq") * lax.axis_size("fsdp")
    grad_scale = 1.0 / math.sqrt(total_patches)
    first_panel = lax.axis_index("fsdp") * jnp.int32(panel_rows)
    row_index = first_panel + jnp.arange(panel_rows, dtype=jnp.int32)
    flat_index = (
        row_index[:, None] * jnp.int32(row_width) + jnp.arange(row_width, dtype=jnp.int32)[None, :]
    )
    dither_noise = mix_bits(flat_index, round_seed[0], step_count[0])
    grad_proj = proj_sum * grad_scale + QUANT * (dither_noise - 0.5)
    return (grad_bytes, grad_proj, conv_sum * grad_scale, gain_sum * grad_scale)


def solution(mesh):
    in_specs = (
        P("fsdp", "seq", None),
        P("fsdp", "seq", None),
        P("fsdp", "seq"),
        P(),
        P(),
        P("fsdp", None),
        P(),
        P(),
    )
    out_specs = (P("fsdp", "seq", None), P("fsdp", None), P(), P())
    return jax.shard_map(
        per_device, mesh=mesh, in_specs=in_specs, out_specs=out_specs, check_vma=False
    )
```

profile of v0, /device:TPU:32, one launch (start us, length us, event | category | flops | bytes accessed | tf_op | source)
XLA Modules:
  0.0 572.1 jit_solution(2157465076530851833)
XLA Ops:
  7.2 0.7 all-gather.2.cloned.1.call-update
  7.9 0.7 slice_bitcast_fusion.2
  8.6 1.3 collective-permute-start.1
  9.9 0.7 slice_bitcast_fusion.1
  10.6 1.3 collective-permute-start
  11.9 0.7 slice_bitcast_fusion
  12.6 1.3 collective-permute-start.2
  13.9 9.7 %concatenate.46 = bf16[256,4,32,16]{3,2,1,0:T(8,128)(2,1)} reshape(bf16[1,1024,512]{2,1,0:T(8,128)(2,1)} %param.8) | data formatting | bytes 2097152 | tf_op jit(solution)/shard_map/concatenate | solution.py:51
  23.6 0.3 reshape_squeeze.2
  23.8 0.5 broadcast.145
  24.4 0.7 reduce.6
  25.0 0.1 concatenate.50
  25.2 9.8 %copy.43 = bf16[256,4,32,16]{0,3,2,1:T(8,128)(2,1)} copy(bf16[256,4,32,16]{3,2,1,0:T(8,128)(2,1)} %concatenate.46) | data formatting | bytes 2097152 | tf_op jit(solution)/shard_map/concatenate | solution.py:51
  35.0 3.1 copy.65
  38.2 0.1 mul.225
  38.2 1.2 copy.49
  39.4 0.1 slice_reduce_fusion
  39.6 0.1 slice.64
  39.8 0.1 fusion.25
  39.9 0.3 pad_maximum_fusion.1
  40.2 8.2 %concatenate.48 = bf16[256,4,32,16]{3,2,1,0:T(8,128)(2,1)} reshape(bf16[1024,512]{1,0:T(8,128)(2,1)S(1)} %pad_maximum_fusion.1) | data formatting | bytes 2097152 | tf_op jit(solution)/shard_map/concatenate | solution.py:51
  48.4 9.8 %copy.44 = bf16[256,4,32,16]{0,3,2,1:T(8,128)(2,1)} copy(bf16[256,4,32,16]{3,2,1,0:T(8,128)(2,1)} %concatenate.48) | data formatting | bytes 2097152 | tf_op jit(solution)/shard_map/concatenate | solution.py:51
  58.2 0.2 pad_maximum_fusion
  58.5 0.3 reshape.239
  58.8 1.2 copy.50
  60.0 0.2 copy-done.6
  60.2 0.5 copy-done.7
  60.7 0.2 maximum_multiply_fusion
  60.9 1.0 copy-done.8
  61.9 0.8 fusion.21
  62.7 0.8 copy-done.4
  63.5 0.1 fusion.23
  63.6 7.9 %fusion.6 = bf16[256,8,512]{2,0,1:T(8,128)(2,1)} fusion(bf16[256,512,1]{0,1,2:T(8,128)(2,1)S(1)} %bitcast.62, bf16[8,512,512]{2,1,0:T(8,128)(2,1)} %bitcast.67, bf16[256,4,512]{2,0,1:T(8,128)(2,1)} %copy.50, bf16[256,4,512]{2,0,1:T(8,128)(2,1)} %copy.49, f32[256,8]{0,1:T(8,128)S(1)} %get-tuple-element.18), kind=kOutput, calls=%fused_computation.8 | convolution fusion | flops 1096810496 | bytes 8658944 | tf_op jit(solution)/shard_map/dot_general | solution.py:86
  71.5 3.9 copy.52
  75.4 6.1 %fusion.27 = f32[4096,512]{1,0:T(8,128)} fusion(bf16[256,4096]{0,1:T(8,128)(2,1)} %bitcast.55, bf16[256,512]{0,1:T(8,128)(2,1)S(1)} %bitcast.63), kind=kOutput, calls=%fused_computation.54 | convolution fusion | flops 1073741824 | bytes 10747904 | tf_op jit(solution)/shard_map/dot_general | solution.py:96
  81.6 0.2 all-reduce.5.cloned.1.call-start
  81.8 3.5 copy.56
  86.6 2.0 copy.53
  88.7 4.3 multiply_reduce_fusion
  93.1 1.0 multiply_subtract_fusion
  94.0 2.0 copy.55
  96.1 3.2 convolution_bitcast_fusion
  99.2 2.6 copy.57
  101.8 5.4 copy.58
  107.2 2.6 broadcast_multiply_fusion
  109.8 2.0 copy-done
  111.8 5.8 %collective-permute-start.3 = (f32[4,512]{1,0:T(4,128)S(1)}, f32[4,512]{1,0:T(4,128)S(1)}, u32[]{:S(2)}, u32[]{:S(2)}) collective-permute-start(f32[4,512]{1,0:T(4,128)S(1)} %bitcast.65), channel_id=1, source_target_pairs={{0,16},{16,32},{32,48},{48,64},{64,80},{80,96},{96,112},{112,128},... | collective-permute-start | bytes 24584 | tf_op jit(solution)/shard_map/ppermute | solution.py:22
  117.6 82.1 %psum.23 = f32[512]{0:T(512)S(1)} all-reduce(f32[512]{0:T(512)S(1)} %get-tuple-element.16), channel_id=1, replica_groups=mesh['seq'=16,'fsdp'=16] {'seq','fsdp'}, use_global_device_ids=true, to_apply=%region_6.0 | all-reduce | flops 512 | bytes 4096 | tf_op jit(solution)/shard_map/psum | solution.py:113
  199.7 9.8 %fusion.10 = f32[8,32,16,16]{2,3,0,1:T(8,128)} fusion(f32[256,32,16,1]{0,2,3,1:T(8,128)} %bitcast.60, bf16[256,8,32,16]{0,3,2,1:T(8,128)(2,1)S(1)} %maximum_multiply_fusion), kind=kOutput, calls=%fused_computation.16 | convolution fusion | flops 201326592 | bytes 2883584 | tf_op jit(solution)/shard_map/pkgc,pgd->kgcd/dot_general | solution.py:110
  209.5 0.3 all-reduce.3.cloned.1.call-start
  209.8 0.6 broadcast_multiply_fusion.2
  210.4 2.2 copy-done.1
  212.6 0.2 slice.77
  212.7 1.4 slice-done
  214.2 2.7 copy.59
  216.8 2.9 reshape.243
  219.8 2.7 copy.60
  222.4 3.1 concatenate.56
  225.6 3.5 fusion.7
  229.1 234.9 %all-reduce.5.cloned.1.call-done = f32[8,32,16,16]{2,3,0,1:T(8,128)} async-done(((f32[8,32,16,16]{2,3,0,1:T(8,128)}), f32[8,32,16,16]{2,3,0,1:T(8,128)}) %all-reduce.5.cloned.1.call-update) | async-done | bytes 262160 | tf_op jit(solution)/shard_map/psum | solution.py:113
  464.1 1.8 broadcast_multiply_fusion.1
  465.8 2.3 copy.63
  468.1 95.2 %all-reduce.3.cloned.1.call-done = f32[256,512]{1,0:T(8,128)} async-done(((f32[256,512]{1,0:T(8,128)}), f32[256,512]{1,0:T(8,128)}) %all-reduce.3.cloned.1.call-update) | async-done | bytes 524304 | tf_op jit(solution)/shard_map/psum | solution.py:101
  563.3 2.2 fusion.20
  (41 shorter events, 0.5 us)
Async XLA Ops:
  7.2 56.5 %all-gather.2.cloned.1.call-start = ((), (), s32[]{:S(2)}) async-start(), calls=%async_computation.1 | async-start | bytes 4456448 | tf_op jit(solution)/shard_map/all_gather | solution.py:85
  7.9 217.7 %reduce-scatter.2.cloned.1.call-start = ((), (), s32[]{:S(2)}) async-start(), calls=%async_computation.2 | async-start | bytes 8912896 | tf_op jit(solution)/shard_map/reduce_scatter | solution.py:95
  8.6 30.9 %collective-permute-start.1 = (s32[4]{0:T(128)S(1)}, s32[4]{0:T(128)S(1)}, u32[]{:S(2)}, u32[]{:S(2)}) collective-permute-start(s32[4]{0:T(128)S(1)} %slice_bitcast_fusion.2), channel_id=1, source_target_pairs={{16,0},{32,16},{48,32},{64,48},{80,64},{96,80},{112,96},{128,112},... | collective-permute-start | bytes 56 | tf_op jit(solution)/shard_map/ppermute | solution.py:22
  10.6 29.3 %collective-permute-start = (bf16[4,512]{1,0:T(4,128)(2,1)S(1)}, bf16[4,512]{1,0:T(4,128)(2,1)S(1)}, u32[]{:S(2)}, u32[]{:S(2)}) collective-permute-start(bf16[4,512]{1,0:T(4,128)(2,1)S(1)} %slice_bitcast_fusion.1), channel_id=1, source_target_pairs={{16,0},{32,16},{48,32},{64,48},{80,64},{96,80},{112,96},{128,112},... | collective-permute-start | bytes 12296 | tf_op jit(solution)/shard_map/ppermute | solution.py:22
  12.6 45.6 %collective-permute-start.2 = (bf16[4,512]{1,0:T(4,128)(2,1)S(1)}, bf16[4,512]{1,0:T(4,128)(2,1)S(1)}, u32[]{:S(2)}, u32[]{:S(2)}) collective-permute-start(bf16[4,512]{1,0:T(4,128)(2,1)S(1)} %slice_bitcast_fusion), channel_id=1, source_target_pairs={{16,0},{32,16},{48,32},{64,48},{80,64},{96,80},{112,96},{128,112},... | collective-permute-start | bytes 12296 | tf_op jit(solution)/shard_map/ppermute | solution.py:22
  13.9 9.7 %copy-start.2 = (bf16[1,1024,512]{2,1,0:T(8,128)(2,1)S(1)}, bf16[1,1024,512]{2,1,0:T(8,128)(2,1)}, u32[]{:S(2)}) copy-start(bf16[1,1024,512]{2,1,0:T(8,128)(2,1)} %param.9) | copy-start | bytes 3145732
  23.6 0.8 copy-start.10
  25.2 12.9 %copy-start.11 = (f32[512]{0:T(512)S(1)}, f32[512]{0:T(512)}, u32[]{:S(2)}) copy-start(f32[512]{0:T(512)} %param.12) | copy-start | bytes 6148
  35.0 4.9 copy-start.5
  58.8 1.4 copy-start.6
  58.8 1.9 copy-start.7
  60.7 1.2 copy-start.8
  62.7 0.8 copy-start.4
  81.6 382.5 %all-reduce.5.cloned.1.call-start = ((), (), s32[]{:S(2)}) async-start(), calls=%async_computation.4 | async-start | bytes 4194304 | tf_op jit(solution)/shard_map/psum | solution.py:113
  88.7 4.4 copy-start.9
  109.8 2.0 copy-start
  111.8 113.8 %collective-permute-start.3 = (f32[4,512]{1,0:T(4,128)S(1)}, f32[4,512]{1,0:T(4,128)S(1)}, u32[]{:S(2)}, u32[]{:S(2)}) collective-permute-start(f32[4,512]{1,0:T(4,128)S(1)} %bitcast.65), channel_id=1, source_target_pairs={{0,16},{16,32},{32,48},{48,64},{64,80},{80,96},{96,112},{112,128},... | collective-permute-start | bytes 24584 | tf_op jit(solution)/shard_map/ppermute | solution.py:22
  209.5 353.8 %all-reduce.3.cloned.1.call-start = ((), (), s32[]{:S(2)}) async-start(), calls=%async_computation.3 | async-start | bytes 1048576 | tf_op jit(solution)/shard_map/psum | solution.py:101
  210.4 2.2 copy-start.1
  212.6 1.6 slice-start
  222.4 3.2 copy-start.3
Sparse Core Ops, SparseCore 0:
  9.8 44.4 all-gather.1
  81.7 75.4 reduce-scatter.1
  209.6 254.3 all-reduce.4
  467.1 96.1 all-reduce.2
where the time goes:
time: 574 us; the launch traced here: 572 us
  waiting for transfers between devices  331 us (58%)
  local copies, waits for them, and re-layouts  88.1 us (15%)
  blocking collectives  82.1 us (14%)
  matrix products  32.1 us (6%)
  between operations  15.3 us (3%)
  other arithmetic  13.3 us (2%)
  starting transfers between devices  10.2 us (2%)
    psum x1, waiting for transfers between devices, per_device(): gain_sum, conv_sum = lax.psum((gain_part, conv_part), ('seq', 'fsdp'))  235 us
    psum x1, waiting for transfers between devices, per_device(): proj_sum = lax.psum(panel_part, 'seq')  95.2 us
    psum x1, blocking collectives, per_device(): gain_sum, conv_sum = lax.psum((gain_part, conv_part), ('seq', 'fsdp'))  82.1 us
    concatenate x6, local copies, waits for them, and re-layouts, tap_windows(): return jnp.concatenate([lower, upper], 1)  37.7 us
    unnamed x29, local copies, waits for them, and re-layouts  16.2 us
  transfers between devices with their start and end apart: 8, of which 2 were waited for; matrix products, arithmetic and copies ran while one was open for 18% of the time, Pallas kernels for 0%

commit v1 on v0

v1 whole, which is shorter than its diff:
```python
import math

import jax
import jax.numpy as jnp
from jax import lax
from jax.sharding import PartitionSpec as P

GROUPS = 32
KERNEL = 8
STRIDE = 4
CG = 16


GELU_A = 0.7978845608028654
GELU_B = 0.044715
QUANT = 0.25


def shifted(value, axis, steps):
    count = lax.axis_size(axis)
    initial, last = (max(0, -steps), min(count, count - steps))
    return lax.ppermute(value, axis, [(source, source + steps) for source in range(initial, last)])


def gelu_grad(values):
    tangent = jnp.tanh(GELU_A * (values + GELU_B * values * values * values))
    return 0.5 * (1.0 + tangent) + 0.5 * values * (1.0 - tangent * tangent) * GELU_A * (
        1.0 + 3.0 * GELU_B * values * values
    )


def mix_bits(flat_index, seed_value, step_value):
    hashed = (
        flat_index * jnp.int32(-1640531535)
        + seed_value * jnp.int32(-2048144777)
        + step_value * jnp.int32(-1028477379)
    )
    hashed = hashed ^ lax.shift_right_logical(hashed, jnp.int32(16))
    hashed = hashed * jnp.int32(2146121005)
    hashed = hashed ^ lax.shift_right_logical(hashed, jnp.int32(15))
    hashed = hashed * jnp.int32(-2073254261)
    hashed = hashed ^ lax.shift_right_logical(hashed, jnp.int32(16))
    return lax.shift_right_logical(hashed, jnp.int32(8)).astype(jnp.float32) / 16777216.0


def split_bf16(value):
    high = value.astype(jnp.bfloat16)
    low = (value - high.astype(jnp.float32)).astype(jnp.bfloat16)
    return high, low


def dot_f32(lhs, rhs, dims):
    return lax.dot_general(lhs, rhs, (dims, ((), ())), preferred_element_type=jnp.float32)


def per_device(
    byte_rows, cotangent, doc_ids, conv_weight, norm_gain, proj_weight, round_seed, step_count
):
    byte_block = byte_rows[0]
    upstream = cotangent[0]
    doc_block = doc_ids[0]
    length = byte_block.shape[0]
    row_width = byte_block.shape[1]
    patches = length // STRIDE
    half = STRIDE * row_width
    panel_rows = proj_weight.shape[0]
    next_bytes, next_up, next_docs = shifted(
        (byte_block[:STRIDE], upstream[:STRIDE], doc_block[:STRIDE]), "seq", -1
    )
    bytes_lo = byte_block.reshape(patches, half)
    bytes_hi = jnp.concatenate([bytes_lo[1:], next_bytes.reshape(1, half)], 0)
    up_lo = upstream.reshape(patches, half)
    up_hi = jnp.concatenate([up_lo[1:], next_up.reshape(1, half)], 0)
    docs_lo = doc_block.reshape(patches, STRIDE)
    docs_hi = jnp.concatenate([docs_lo[1:], next_docs.reshape(1, STRIDE)], 0)
    is_last = lax.axis_index("seq") == lax.axis_size("seq") - 1
    patch_ids = lax.broadcasted_iota(jnp.int32, (patches, STRIDE), 0)
    spilled = is_last & (patch_ids == patches - 1)
    keep_lo = docs_lo == docs_lo[:, :1]
    keep_hi = (docs_hi == docs_lo[:, :1]) & jnp.logical_not(spilled)

    def spread(keep):
        return jnp.broadcast_to(keep[:, :, None], (patches, STRIDE, row_width)).reshape(
            patches, half
        )

    keep_lo_f = spread(keep_lo.astype(jnp.float32))
    keep_hi_f = spread(keep_hi.astype(jnp.float32))
    win_lo = bytes_lo * keep_lo_f.astype(jnp.bfloat16)
    win_hi = bytes_hi * keep_hi_f.astype(jnp.bfloat16)

    group_eye = jnp.eye(GROUPS, dtype=jnp.bfloat16)
    dense_weight = (
        conv_weight[:, :, :, None, :] * group_eye[None, :, None, :, None]
    ).reshape(KERNEL, row_width, row_width)
    weight_lo = dense_weight[:STRIDE].reshape(half, row_width)
    weight_hi = dense_weight[STRIDE:].reshape(half, row_width)

    hidden = dot_f32(win_lo, weight_lo, ((1,), (0,))) + dot_f32(win_hi, weight_hi, ((1,), (0,)))
    factor = lax.rsqrt(jnp.mean(hidden * hidden, axis=-1, keepdims=True) + 1e-06)
    normed = (hidden * factor * norm_gain).astype(jnp.bfloat16)

    full_proj = lax.all_gather(proj_weight, "fsdp", axis=0, tiled=True)
    proj_lo = full_proj[:half]
    proj_hi = full_proj[half:]
    pre_lo = dot_f32(normed, proj_lo, ((1,), (1,)))
    pre_hi = dot_f32(normed, proj_hi, ((1,), (1,)))
    grad_pre_lo = (up_lo.astype(jnp.float32) * keep_lo_f * gelu_grad(pre_lo)).astype(jnp.bfloat16)
    grad_pre_hi = (up_hi.astype(jnp.float32) * keep_hi_f * gelu_grad(pre_hi)).astype(jnp.bfloat16)

    proj_part = jnp.concatenate(
        [dot_f32(grad_pre_lo, normed, ((0,), (0,))), dot_f32(grad_pre_hi, normed, ((0,), (0,)))], 0
    )
    panel_part = lax.psum_scatter(proj_part, "fsdp", scatter_dimension=0, tiled=True)

    grad_norm = dot_f32(grad_pre_lo, proj_lo, ((1,), (0,))) + dot_f32(
        grad_pre_hi, proj_hi, ((1,), (0,))
    )
    gain_part = jnp.sum(grad_norm * hidden * factor, axis=0)
    gained = norm_gain * grad_norm
    grad_hidden = factor * gained - hidden * factor * factor * factor * jnp.mean(
        gained * hidden, axis=-1, keepdims=True
    )
    gh_high, gh_low = split_bf16(grad_hidden)

    def window_grad(window):
        full = dot_f32(window, gh_high, ((0,), (0,))) + dot_f32(window, gh_low, ((0,), (0,)))
        blocks = full.reshape(STRIDE, GROUPS, CG, GROUPS, CG)
        mask = jnp.eye(GROUPS, dtype=jnp.float32)[None, :, None, :, None]
        return jnp.sum(blocks * mask, axis=3)

    conv_part = jnp.concatenate([window_grad(win_lo), window_grad(win_hi)], 0)

    def back_taps(weight, keep_f):
        taps = dot_f32(gh_high, weight, ((1,), (1,))) + dot_f32(gh_low, weight, ((1,), (1,)))
        return (taps * keep_f).reshape(length, row_width)

    back_lower = back_taps(weight_lo, keep_lo_f)
    back_upper = back_taps(weight_hi, keep_hi_f)
    incoming = shifted(back_upper[length - STRIDE :], "seq", 1)
    back_rows = back_lower + jnp.concatenate([incoming, back_upper[: length - STRIDE]], 0)
    grad_bytes = (upstream.astype(jnp.float32) + back_rows)[None]

    conv_size = conv_part.size
    small = jnp.concatenate([conv_part.reshape(-1), gain_part]).reshape(-1, row_width)
    small = lax.psum(small, "fsdp")
    joined = lax.psum(jnp.concatenate([panel_part, small], 0), "seq")
    proj_sum = joined[:panel_rows]
    small_sum = joined[panel_rows:].reshape(-1)
    conv_sum = small_sum[:conv_size].reshape(conv_part.shape)
    gain_sum = small_sum[conv_size:]

    total_patches = patches * lax.axis_size("seq") * lax.axis_size("fsdp")
    grad_scale = 1.0 / math.sqrt(total_patches)
    first_panel = lax.axis_index("fsdp") * jnp.int32(panel_rows)
    row_index = first_panel + jnp.arange(panel_rows, dtype=jnp.int32)
    flat_index = (
        row_index[:, None] * jnp.int32(row_width) + jnp.arange(row_width, dtype=jnp.int32)[None, :]
    )
    dither_noise = mix_bits(flat_index, round_seed[0], step_count[0])
    grad_proj = proj_sum * grad_scale + QUANT * (dither_noise - 0.5)
    return (grad_bytes, grad_proj, conv_sum * grad_scale, gain_sum * grad_scale)


def solution(mesh):
    in_specs = (
        P("fsdp", "seq", None),
        P("fsdp", "seq", None),
        P("fsdp", "seq"),
        P(),
        P(),
        P("fsdp", None),
        P(),
        P(),
    )
    out_specs = (P("fsdp", "seq", None), P("fsdp", None), P(), P())
    return jax.shard_map(
        per_device, mesh=mesh, in_specs=in_specs, out_specs=out_specs, check_vma=False
    )
```

time: 574 us -> 529 us (0.922)
  waiting for transfers between devices: 331 us -> 247 us
  blocking collectives: 82.1 us -> 0 us
  local copies, waits for them, and re-layouts: 88.1 us -> 161 us
  other arithmetic: 13.3 us -> 59.2 us
    psum x2, waiting for transfers between devices: 330 us -> 176 us  [the longest x1 89.3 us: per_device(): small = lax.psum(small, 'fsdp')]
    reshape x5 -> x7, local copies, waits for them, and re-layouts: 11.8 us -> 103 us  [the longest x2 39.7 us: window_grad(): blocks = full.reshape(STRIDE, GROUPS, CG, GROUPS, CG)]
    psum x1 -> x0, blocking collectives: 82.1 us -> none  [per_device(): gain_sum, conv_sum = lax.psum((gain_part, conv_part), ('seq', 'fsdp'))]
    reduce_scatter x1, waiting for transfers between devices: 0.01 us -> 71 us  [per_device(): lax.psum_scatter(proj_part, 'fsdp', scatter_dimension=0, tiled=True)]
    concatenate x6 -> x4, local copies, waits for them, and re-layouts: 37.7 us -> 1.79 us  [the longest x1 1.49 us: per_device(): bytes_hi = jnp.concatenate([bytes_lo[1:], next_bytes.reshape(1, half)], 0)]
    reduce_sum x0 -> x1, other arithmetic: none -> 25.5 us  [window_grad(): return jnp.sum(blocks * mask, axis=3)]
    slice x8 -> x7, local copies, waits for them, and re-layouts: 7.23 us -> 32.6 us  [the longest x1 25.7 us: per_device(): weight_hi = dense_weight[STRIDE:].reshape(half, row_width)]
    concatenate x3 -> x4, other arithmetic: 0.57 us -> 12.5 us  [the longest x1 7.67 us: per_device(): jnp.concatenate([dot_f32(grad_pre_lo, normed, ((0,), (0,))), dot_f32(grad...]
  transfers between devices with their start and end apart: 8 -> 8, of which waited for: 2 -> 3; matrix products, arithmetic and copies ran while one was open for 18% -> 28% of each run, Pallas kernels for 0% -> 0%
where the time goes in v1:
time: 529 us; the launch traced here: 527 us
  waiting for transfers between devices  247 us (47%)
  local copies, waits for them, and re-layouts  161 us (30%)
  other arithmetic  59.2 us (11%)
  matrix products  34.6 us (7%)
  between operations  15.6 us (3%)
  starting transfers between devices  9.79 us (2%)
    psum x1, waiting for transfers between devices, per_device(): small = lax.psum(small, 'fsdp')  89.3 us
    psum x1, waiting for transfers between devices, per_device(): joined = lax.psum(jnp.concatenate([panel_part, small], 0), 'seq')  86.9 us
    reduce_scatter x1, waiting for transfers between devices, per_device(): lax.psum_scatter(proj_part, 'fsdp', scatter_dimension=0, tiled=True)  71 us
    reshape x2, local copies, waits for them, and re-layouts, window_grad(): blocks = full.reshape(STRIDE, GROUPS, CG, GROUPS, CG)  39.7 us
    dot_general x16, matrix products, dot_f32(): lax.dot_general(lhs, rhs, (dims, ((), ())), preferred_element_type=jnp.fl...  34.6 us
    reshape x1, local copies, waits for them, and re-layouts, per_device(): weight_lo = dense_weight[:STRIDE].reshape(half, row_width)  28.7 us
    reshape x1, local copies, waits for them, and re-layouts, per_device(): weight_hi = dense_weight[STRIDE:].reshape(half, row_width)  28.2 us
    slice x1, local copies, waits for them, and re-layouts, per_device(): weight_hi = dense_weight[STRIDE:].reshape(half, row_width)  25.7 us
  transfers between devices with their start and end apart: 8, of which 3 were waited for; matrix products, arithmetic and copies ran while one was open for 28% of the time, Pallas kernels for 0%

profile of v1, /device:TPU:32, one launch (start us, length us, event | category | flops | bytes accessed | tf_op | source)
XLA Modules:
  0.0 527.3 jit_solution(15065183540422117678)
XLA Ops:
  7.2 0.7 slice_bitcast_fusion.2
  8.0 1.3 collective-permute-start.1
  9.2 0.7 slice_bitcast_fusion.1
  10.0 1.3 collective-permute-start
  11.2 0.7 slice_bitcast_fusion
  11.9 1.3 collective-permute-start.2
  13.8 1.3 reduce.13
  15.4 0.8 slice_reduce_fusion.2
  16.3 1.5 slice.78
  17.8 1.2 slice.86
  19.0 1.6 reshape.263
  20.6 1.4 reshape_squeeze.11
  22.0 1.5 concatenate.56
  23.5 1.7 slice.94
  25.9 1.5 mul.283
  27.3 0.8 copy.23
  28.2 11.2 %broadcast_multiply_fusion = bf16[8,32,16,32,16]{4,3,2,1,0:T(8,128)(2,1)} fusion(bf16[32,32]{1,0:T(8,128)(2,1)S(1)} %fusion.39, bf16[8,32,16,16]{3,2,1,0:T(8,128)(2,1)S(1)} %copy.23), kind=kLoop, calls=%fused_computation.2 | loop fusion | flops 2097152 | bytes 4327424 | tf_op jit(solution)/shard_map/mul | solution.py:94
  39.4 25.7 %fusion.44 = (bf16[4,32,16,32,16]{4,3,2,1,0:T(8,128)(2,1)}, bf16[4,32,16,32,16]{4,3,2,1,0:T(8,128)(2,1)}) fusion(bf16[8,32,16,32,16]{4,3,2,1,0:T(8,128)(2,1)} %broadcast_multiply_fusion), kind=kLoop, calls=%fused_computation.87 | loop fusion | bytes 8388608 | tf_op jit(solution)/shard_map/slice | solution.py:97
  65.1 28.7 %reshape.252 = bf16[2048,512]{1,0:T(8,128)(2,1)} reshape(bf16[4,32,16,32,16]{4,3,2,1,0:T(8,128)(2,1)} %get-tuple-element.29) | data formatting | bytes 4194304 | tf_op jit(solution)/shard_map/reshape | solution.py:96
  93.8 28.2 %reshape.253 = bf16[2048,512]{1,0:T(8,128)(2,1)S(1)} reshape(bf16[4,32,16,32,16]{4,3,2,1,0:T(8,128)(2,1)} %get-tuple-element.28) | data formatting | bytes 4194304 | tf_op jit(solution)/shard_map/reshape | solution.py:97
  122.0 1.6 slice.87
  123.6 2.6 fusion.45
  126.9 2.2 copy.32
  129.8 0.9 copy.34
  131.0 0.8 maximum_multiply_fusion
  132.2 0.8 multiply_reduce_fusion.4
  133.1 0.6 copy-done.12
  134.1 4.3 fusion.15
  138.5 2.9 fusion.49
  141.8 1.6 copy-done.22
  143.4 1.8 fusion.8
  145.2 2.7 fusion.48
  148.0 0.7 fusion.17
  149.0 0.9 multiply_reduce_fusion.2
  150.1 1.1 copy-done.7
  151.2 1.0 fusion.40
  152.2 2.8 convolution_add_fusion.1
  155.1 19.8 %reshape.258 = f32[4,32,16,32,16]{4,3,2,1,0:T(8,128)} reshape(f32[2048,512]{1,0:T(8,128)} %convolution_add_fusion.1) | data formatting | bytes 8388608 | tf_op jit(solution)/shard_map/reshape | solution.py:128
  174.9 1.7 fusion.50
  176.6 2.8 convolution_add_fusion
  179.4 19.8 %reshape.260 = f32[4,32,16,32,16]{4,3,2,1,0:T(8,128)} reshape(f32[2048,512]{1,0:T(8,128)} %convolution_add_fusion) | data formatting | bytes 8388608 | tf_op jit(solution)/shard_map/reshape | solution.py:128
  199.2 25.5 %multiply_reduce_fusion.1 = (f32[4,32,16,16]{3,2,1,0:T(8,128)S(1)}, f32[4,32,16,16]{3,2,1,0:T(8,128)}) fusion(f32[4,32,16,32,16]{4,3,2,1,0:T(8,128)} %reshape.258, f32[32,32]{1,0:T(8,128)S(1)} %fusion.38, f32[4,32,16,32,16]{4,3,2,1,0:T(8,128)} %reshape.260), kind=kLoop, calls=%fused_computation.1 | loop fusion | flops 4128768 | bytes 8654848 | tf_op jit(solution)/shard_map/reduce_sum | solution.py:130
  224.7 2.7 pad_maximum_fusion.1
  227.5 2.2 reshape.261
  229.7 0.7 reshape.262
  230.5 7.7 %pad_maximum_fusion = f32[4096,512]{1,0:T(8,128)} fusion(f32[2048,512]{1,0:T(8,128)} %fusion.49, f32[2048,512]{1,0:T(8,128)} %fusion.48), kind=kLoop, calls=%fused_computation.3 | loop fusion | flops 2097152 | bytes 16777216 | tf_op jit(solution)/shard_map/concatenate | solution.py:111
  239.6 0.7 fusion.47
  240.3 0.8 copy-done.3
  241.2 0.8 fusion
  242.0 1.4 copy-done.8
  243.4 5.8 %collective-permute-start.3 = (f32[4,512]{1,0:T(4,128)S(1)}, f32[4,512]{1,0:T(4,128)S(1)}, u32[]{:S(2)}, u32[]{:S(2)}) collective-permute-start(f32[4,512]{1,0:T(4,128)S(1)} %slice.92), channel_id=1, source_target_pairs={{0,16},{16,32},{32,48},{48,64},{64,80},{80,96},{96,112},{112,128},... | collective-permute-start | bytes 24584 | tf_op jit(solution)/shard_map/ppermute | solution.py:22
  249.2 3.7 fusion.46
  252.9 89.3 %all-reduce.3.cloned.1.call-done = f32[129,512]{1,0:T(8,128)} async-done(((f32[129,512]{1,0:T(8,128)}), f32[129,512]{1,0:T(8,128)}) %all-reduce.3.cloned.1.call-update) | async-done | bytes 264208 | tf_op jit(solution)/shard_map/psum | solution.py:146
  342.1 71.0 %reduce-scatter.2.cloned.1.call-done = f32[256,512]{1,0:T(8,128)} async-done(((f32[4096,512]{1,0:T(8,128)}), f32[256,512]{1,0:T(8,128)}) %reduce-scatter.2.cloned.1.call-update) | async-done | bytes 524304 | tf_op jit(solution)/shard_map/reduce_scatter | solution.py:114
  413.2 2.1 pad_maximum_fusion.2
  415.3 4.3 fusion.1
  419.6 3.0 reshape.257
  422.6 1.9 concatenate.64
  424.5 4.1 fusion.16
  428.6 86.9 %all-reduce.5.cloned.1.call-done = f32[385,512]{1,0:T(8,128)} async-done(((f32[385,512]{1,0:T(8,128)}), f32[385,512]{1,0:T(8,128)}) %all-reduce.5.cloned.1.call-update) | async-done | bytes 788496 | tf_op jit(solution)/shard_map/psum | solution.py:147
  515.5 1.0 slice_multiply_fusion.1
  516.5 0.7 mul.357
  517.2 1.8 copy.30
  519.6 1.2 fusion.37
  (87 shorter events, 5.7 us)
Async XLA Ops:
  7.2 10.6 %copy-start.5 = (bf16[1,1024,512]{2,1,0:T(8,128)(2,1)S(1)}, bf16[1,1024,512]{2,1,0:T(8,128)(2,1)}, u32[]{:S(2)}) copy-start(bf16[1,1024,512]{2,1,0:T(8,128)(2,1)} %param.9) | copy-start | bytes 3145732
  7.2 126.9 %all-gather.2.cloned.1.call-start = ((), (), s32[]{:S(2)}) async-start(), calls=%async_computation.1 | async-start | bytes 4456448 | tf_op jit(solution)/shard_map/all_gather | solution.py:103
  8.0 118.3 %collective-permute-start.1 = (s32[4]{0:T(128)S(1)}, s32[4]{0:T(128)S(1)}, u32[]{:S(2)}, u32[]{:S(2)}) collective-permute-start(s32[4]{0:T(128)S(1)} %slice_bitcast_fusion.2), channel_id=1, source_target_pairs={{16,0},{32,16},{48,32},{64,48},{80,64},{96,80},{112,96},{128,112},... | collective-permute-start | bytes 56 | tf_op jit(solution)/shard_map/ppermute | solution.py:22
  10.0 120.7 %collective-permute-start = (bf16[4,512]{1,0:T(4,128)(2,1)S(1)}, bf16[4,512]{1,0:T(4,128)(2,1)S(1)}, u32[]{:S(2)}, u32[]{:S(2)}) collective-permute-start(bf16[4,512]{1,0:T(4,128)(2,1)S(1)} %slice_bitcast_fusion.1), channel_id=1, source_target_pairs={{16,0},{32,16},{48,32},{64,48},{80,64},{96,80},{112,96},{128,112},... | collective-permute-start | bytes 12296 | tf_op jit(solution)/shard_map/ppermute | solution.py:22
  11.9 120.2 %collective-permute-start.2 = (bf16[4,512]{1,0:T(4,128)(2,1)S(1)}, bf16[4,512]{1,0:T(4,128)(2,1)S(1)}, u32[]{:S(2)}, u32[]{:S(2)}) collective-permute-start(bf16[4,512]{1,0:T(4,128)(2,1)S(1)} %slice_bitcast_fusion), channel_id=1, source_target_pairs={{16,0},{32,16},{48,32},{64,48},{80,64},{96,80},{112,96},{128,112},... | collective-permute-start | bytes 12296 | tf_op jit(solution)/shard_map/ppermute | solution.py:22
  13.3 328.9 %all-reduce.3.cloned.1.call-start = ((), (), s32[]{:S(2)}) async-start(), calls=%async_computation.3 | async-start | bytes 557056 | tf_op jit(solution)/shard_map/psum | solution.py:146
  19.0 1.6 copy-start.4
  22.0 3.6 copy-start.20
  25.7 1.7 copy-start.19
  93.8 28.2 %copy-start.14 = (bf16[1,1020,512]{2,1,0:T(8,128)(2,1)S(1)}, bf16[1,1020,512]{2,1,0:T(8,128)(2,1)}, u32[]{:S(2)}) copy-start(bf16[1,1020,512]{2,1,0:T(8,128)(2,1)} %slice.86) | copy-start | bytes 3133444
  129.8 1.2 copy-start.16
  130.7 3.1 copy-start.2
  132.1 0.8 copy-start.21
  132.2 1.6 copy-start.15
  133.0 0.8 copy-start.12
  138.4 2.9 copy-start
  138.4 3.4 copy-start.17
  138.5 5.0 copy-start.22
  148.0 1.0 copy-start.13
  149.9 1.3 copy-start.7
  150.1 2.1 copy-start.10
  230.4 182.7 %reduce-scatter.2.cloned.1.call-start = ((), (), s32[]{:S(2)}) async-start(), calls=%async_computation.2 | async-start | bytes 8912896 | tf_op jit(solution)/shard_map/reduce_scatter | solution.py:114
  238.2 1.4 copy-start.11
  238.2 277.3 %all-reduce.5.cloned.1.call-start = ((), (), s32[]{:S(2)}) async-start(), calls=%async_computation.4 | async-start | bytes 1605632 | tf_op jit(solution)/shard_map/psum | solution.py:147
  239.6 1.6 copy-start.3
  242.0 1.4 copy-start.8
  243.4 181.1 %collective-permute-start.3 = (f32[4,512]{1,0:T(4,128)S(1)}, f32[4,512]{1,0:T(4,128)S(1)}, u32[]{:S(2)}, u32[]{:S(2)}) collective-permute-start(f32[4,512]{1,0:T(4,128)S(1)} %slice.92), channel_id=1, source_target_pairs={{0,16},{16,32},{32,48},{48,64},{64,80},{80,96},{96,112},{112,128},... | collective-permute-start | bytes 24584 | tf_op jit(solution)/shard_map/ppermute | solution.py:22
  252.9 162.4 %copy-start.1 = (f32[32,8,4,512]{3,1,2,0:T(8,128)S(1)}, f32[32,8,4,512]{3,1,2,0:T(8,128)}, u32[]{:S(2)}) copy-start(f32[32,8,4,512]{3,1,2,0:T(8,128)} %copy.32) | copy-start | bytes 6291460
  419.6 3.0 copy-start.9
  422.6 1.9 copy-start.6
  517.2 1.8 copy-start.18
Sparse Core Ops, SparseCore 0:
  13.4 50.0 all-gather.1
  230.6 111.5 all-reduce.2
  344.9 68.2 reduce-scatter.1
  417.3 98.1 all-reduce.4
